TPU v7x, 512 devices: a whole 4x8x8 slice. The times are simulated.
512 devices in a mesh: seq: 128 (over z_hi, x, y), dp: 4 (over z_lo, core).
Axes of the slice: x: 4, y: 8, z: 8 (z_hi: 4, z_lo: 2; z = z_hi * 2 + z_lo), core: 2. Of those that a mesh axis runs over, the one named last changes fastest.
Arguments:
- query_proj: bfloat16 [4, 16384, 2048], P('dp', 'seq'), may hold values from -48 to 48
- key_projection: bfloat16 [4, 16384, 1024], P('dp', 'seq'), may hold values from -48 to 48
- value_proj: bfloat16 [4, 16384, 1024], P('dp', 'seq'), may hold values from -6 to 6
- attn_grad: bfloat16 [4, 16384, 2048], P('dp', 'seq'), may hold values from -6 to 6
- doc_ids: int32 [4, 16384], P('dp', 'seq'), may hold values from 0 to 8, as said below
- query_gain: float32 [128], replicated, may hold values from 0.5 to 1.5
- key_norm_gain: float32 [128], replicated, may hold values from 0.5 to 1.5
Outputs:
- query_grad: bfloat16 [4, 16384, 2048], P('dp', 'seq')
- key_grad: bfloat16 [4, 16384, 1024], P('dp', 'seq')
- value_grad: bfloat16 [4, 16384, 1024], P('dp', 'seq')
- query_gain_grad: float32 [128], replicated
- key_gain_grad: float32 [128], replicated
Inputs may be any that keep to these rules, and one draw needn't show every extreme that they name: `doc_ids`: document numbers never fall along a sequence and each is used; each document holds 1 to 2175 tokens, and one holds exactly 2175.
All inputs are finite; a program needn't handle non-finite values.
Results may differ from a plain program's by a relative error of at most 0.008.
Values may be sent and summed in bfloat16 or wider, within the bound.
No kernel may reach another device: no remote copies, remote signals or barrier semaphores. Data moves between devices by JAX's collectives and lax.ppermute only.
A program may use at most 128 MiB of HBM per device.

v0:
```python
import jax
import jax.numpy as jnp
from jax import lax
from jax.sharding import PartitionSpec as P

HEAD_SIZE = 128
QUERY_HEADS = 16
KEY_VALUE_HEADS = 8
WINDOW_LENGTH = 1024
rope_base = 10000.0
score_scale = 168.0 ** (-0.5)
norm_eps = 1e-06


def entering(value, axis, combine, identity):
    length, position = (lax.axis_size(axis), lax.axis_index(axis))
    everything = jax.tree.map(lambda part: lax.all_gather(part, axis), value)
    start = jax.tree.map(
        lambda part, zero: jnp.broadcast_to(jnp.asarray(zero, part.dtype), part.shape),
        value,
        identity,
    )

    def turn(k, before):
        reached = k < position
        new = combine(before, jax.tree.map(lambda part: part[k], everything))
        return jax.tree.map(lambda a, b: jnp.where(reached, a, b), new, before)

    return lax.fori_loop(0, length, turn, start)


def from_behind(value, axis, steps):
    count = lax.axis_size(axis)
    first, last = (max(0, -steps), min(count, count - steps))
    return lax.ppermute(value, axis, [(source, source + steps) for source in range(first, last)])


def rotary(field, positions):
    half = field.shape[-1] // 2
    freqs = rope_base ** (-jnp.arange(half, dtype=field.dtype) * 2.0 / field.shape[-1])
    angles = positions.astype(field.dtype)[:, None] * freqs[None, :]
    cosine = jnp.cos(angles)[:, None, :]
    sine = jnp.sin(angles)[:, None, :]
    first = field[..., :half]
    second = field[..., half:]
    return jnp.concatenate(
        [first * cosine - second * sine, second * cosine + first * sine], axis=-1
    )


def prepare(raw, gain, positions):
    meansq = jnp.mean(raw * raw, axis=-1, keepdims=True)
    normed = raw * lax.rsqrt(meansq + norm_eps) * gain
    return rotary(normed, positions)


def combine_docs(earlier, later):
    vacant = later[0] < 0
    joined = later[0] == earlier[0]
    doc_number = jnp.where(vacant, earlier[0], later[0])
    first_place = jnp.where(vacant | joined, earlier[1], later[1])
    return (doc_number, first_place)


def attend(query_blk, key_blk, value_blk, gradient_block, allowed):
    scores = (
        jnp.einsum("tgrd,wgd->grtw", query_blk, key_blk, preferred_element_type=jnp.float32)
        * score_scale
    )
    expd = jnp.where(allowed, jnp.exp(scores), 0.0)
    weights = expd / jnp.sum(expd, axis=-1, keepdims=True)
    weights_b = weights.astype(jnp.bfloat16)
    attention_probs = jnp.einsum(
        "grtw,wgd->tgrd", weights_b, value_blk, preferred_element_type=jnp.float32
    )
    delta_rows = jnp.einsum("jwkp,jwkp->wkj", gradient_block.astype(jnp.float32), attention_probs)
    dweights = jnp.einsum(
        "tgrd,wgd->grtw", gradient_block, value_blk, preferred_element_type=jnp.float32
    )
    dscores = (weights * (dweights - delta_rows[..., None])).astype(jnp.bfloat16)
    dquery = score_scale * jnp.einsum(
        "grtw,wgd->tgrd", dscores, key_blk, preferred_element_type=jnp.float32
    )
    dkey = score_scale * jnp.einsum(
        "grtw,tgrd->wgd", dscores, query_blk, preferred_element_type=jnp.float32
    )
    dvalue = jnp.einsum(
        "grtw,tgrd->wgd", weights_b, gradient_block, preferred_element_type=jnp.float32
    )
    return (dquery, dkey, dvalue)


def shards(query_proj, key_projection, value_proj, attn_grad, doc_ids, query_gain, key_norm_gain):
    row_count = query_proj.shape[1]
    behind = WINDOW_LENGTH // row_count
    group_ratio = QUERY_HEADS // KEY_VALUE_HEADS
    group_count = KEY_VALUE_HEADS // 2
    key_span_width = KEY_VALUE_HEADS * HEAD_SIZE
    base = lax.axis_index("seq") * row_count
    local = jnp.arange(row_count, dtype=jnp.int32)
    positions = base + local
    doc_row = doc_ids[0]
    same_doc = doc_row[:, None] == doc_row[None, :]
    local_first = jnp.min(jnp.where(same_doc, local[None, :], row_count), axis=1) + base
    carry_doc, carry_start = entering(
        (doc_row[row_count - 1], local_first[row_count - 1]),
        "seq",
        combine_docs,
        (jnp.int32(-1), jnp.int32(0)),
    )
    starts = jnp.where(doc_row == carry_doc, carry_start, local_first)

    def prepare_function(raw, gain):
        return prepare(raw, gain, positions)

    query_normalized, query_back = jax.vjp(
        prepare_function,
        query_proj[0].astype(jnp.float32).reshape(row_count, QUERY_HEADS, HEAD_SIZE),
        query_gain,
    )
    key_normalized, key_backward = jax.vjp(
        prepare_function,
        key_projection[0].astype(jnp.float32).reshape(row_count, KEY_VALUE_HEADS, HEAD_SIZE),
        key_norm_gain,
    )
    query_rot = query_normalized.astype(jnp.bfloat16)
    key_flat = key_normalized.astype(jnp.bfloat16).reshape(row_count, key_span_width)
    value_flat = value_proj[0]
    key_parts = []
    value_parts = []
    for offset in range(behind, 0, -1):
        moved = from_behind((key_flat, value_flat), "seq", offset)
        key_parts.append(moved[0])
        value_parts.append(moved[1])
    key_win = jnp.concatenate(key_parts + [key_flat], axis=0)
    value_win = jnp.concatenate(value_parts + [value_flat], axis=0)
    width = (behind + 1) * row_count
    key_pos = base - behind * row_count + jnp.arange(width, dtype=jnp.int32)
    allowed = (
        (key_pos[None, :] <= positions[:, None])
        & (positions[:, None] - key_pos[None, :] < WINDOW_LENGTH)
        & (key_pos[None, :] >= starts[:, None])
    )
    query_groups = query_rot.reshape(row_count, group_count, 2, group_ratio, HEAD_SIZE).transpose(
        1, 0, 2, 3, 4
    )
    grad_groups = (
        attn_grad[0]
        .reshape(row_count, group_count, 2, group_ratio, HEAD_SIZE)
        .transpose(1, 0, 2, 3, 4)
    )
    key_groups = key_win.reshape(width, group_count, 2, HEAD_SIZE).transpose(1, 0, 2, 3)
    value_groups = value_win.reshape(width, group_count, 2, HEAD_SIZE).transpose(1, 0, 2, 3)

    def group_work(items):
        return attend(items[0], items[1], items[2], items[3], allowed)

    dquery_g, dkey_g, dvalue_g = lax.map(
        group_work, (query_groups, key_groups, value_groups, grad_groups)
    )
    dquery_rot = dquery_g.transpose(1, 0, 2, 3, 4).reshape(row_count, QUERY_HEADS, HEAD_SIZE)
    dkey_win = dkey_g.transpose(1, 0, 2, 3).reshape(behind + 1, row_count, key_span_width)
    dvalue_win = dvalue_g.transpose(1, 0, 2, 3).reshape(behind + 1, row_count, key_span_width)
    key_remote = dkey_win[:behind].astype(jnp.bfloat16)
    value_remote = dvalue_win[:behind].astype(jnp.bfloat16)
    key_full_length = dkey_win[behind]
    value_total = dvalue_win[behind]
    for offset in range(1, behind + 1):
        moved = from_behind(
            (key_remote[behind - offset], value_remote[behind - offset]), "seq", -offset
        )
        key_full_length = key_full_length + moved[0].astype(jnp.float32)
        value_total = value_total + moved[1].astype(jnp.float32)
    query_raw_gradient, query_gain_gradient = query_back(dquery_rot)
    key_raw_gradient, key_gain_gradient = key_backward(
        key_full_length.reshape(row_count, KEY_VALUE_HEADS, HEAD_SIZE)
    )
    gain_query, gain_key = lax.psum((query_gain_gradient, key_gain_gradient), ("seq", "dp"))
    return (
        query_raw_gradient.astype(jnp.bfloat16).reshape(1, row_count, QUERY_HEADS * HEAD_SIZE),
        key_raw_gradient.astype(jnp.bfloat16).reshape(1, row_count, key_span_width),
        value_total.astype(jnp.bfloat16)[None],
        gain_query,
        gain_key,
    )


def solution(mesh):
    in_specs = (
        P("dp", "seq", None),
        P("dp", "seq", None),
        P("dp", "seq", None),
        P("dp", "seq", None),
        P("dp", "seq"),
        P(),
        P(),
    )
    out_specs = (P("dp", "seq", None), P("dp", "seq", None), P("dp", "seq", None), P(), P())
    return jax.shard_map(shards, mesh=mesh, in_specs=in_specs, out_specs=out_specs, check_vma=False)
```

profile of v0, /device:TPU:1, one launch (start us, length us, event | category | flops | bytes accessed | tf_op | source)
XLA Modules:
  0.0 1063.3 jit_solution(8678204765822)
XLA Ops:
  1.8 4.0 collective-permute-start.15
  5.8 4.2 collective-permute-start.14
  10.1 3.1 collective-permute-start.8
  16.6 4.9 collective-permute-start.1
  21.5 2.9 collective-permute-start
  26.4 1.3 bitcast_dynamic-update-slice_fusion
  28.5 28.4 %all-reduce.6 = (s32[128]{0:T(128)S(1)}, s32[128]{0:T(128)S(1)}) all-reduce(s32[128]{0:T(128)S(1)} %bitcast_dynamic-update-slice_fusion, s32[128]{0:T(128)S(1)} %slice_dynamic-update-slice_fusion), channel_id=2, replica_groups=mesh['seq'=128,'dp'=4] {'seq'}, use_global_device_ids=true, to_apply=%add.4 | all-reduce | flops 256 | bytes 2048 | tf_op jit(solution)/shard_map/all_gather | solution.py:17
  57.0 487.3 %while.30 = (s32[]{:T(128)}, s32[]{:T(128)}, s32[]{:T(128)}, s32[]{:T(128)}, s32[128]{0:T(128)S(1)}, /*index=5*/s32[128]{0:T(128)S(1)}, s32[]{:T(128)}, s32[]{:T(128)}) while((s32[]{:T(128)}, s32[]{:T(128)}, s32[]{:T(128)}, s32[]{:T(128)}, s32[128]{0:T(128)S(1)}, /*index=5*/s32[128]{0:T(128)S(1)}, s32[]{:T(128)}, s32[]{:T(128)}) %tuple.77), condition=%wide.region_4.5_spmd, body=%wide.region_3.4_spmd.sunk | while | flops 10 | bytes 199 | solution.py:29
  548.3 9.9 collective-permute-start.2
  559.2 1.3 collective-permute-start.3
  560.5 1.3 collective-permute-start.4
  562.9 7.1 collective-permute-done.2
  571.3 20.7 %collective-permute-done.3 = bf16[128,1024]{0,1:T(8,128)(2,1)S(1)} collective-permute-done((bf16[128,1024]{0,1:T(8,128)(2,1)S(1)}, bf16[128,1024]{0,1:T(8,128)(2,1)S(1)}, u32[]{:S(2)}, u32[]{:S(2)}) %collective-permute-start.3) | collective-permute-done | bytes 262176 | tf_op jit(solution)/shard_map/ppermute | solution.py:35
  593.4 1.3 collective-permute-start.7
  594.8 8.5 collective-permute-start.11
  603.4 10.8 %collective-permute-start.9 = (bf16[128,1024]{0,1:T(8,128)(2,1)S(1)}, bf16[128,1024]{0,1:T(8,128)(2,1)S(1)}, u32[]{:S(2)}, u32[]{:S(2)}) collective-permute-start(bf16[128,1024]{0,1:T(8,128)(2,1)S(1)} %bitcast.260), channel_id=1, source_target_pairs={{0,28},{4,32},{8,36},{12,40},{16,44},{20,48},{24,52},{28,56},{32,6... | collective-permute-start | bytes 786440 | tf_op jit(solution)/shard_map/ppermute | solution.py:35
  615.2 9.4 collective-permute-start.10
  624.7 12.8 %collective-permute-start.12 = (bf16[128,1024]{0,1:T(8,128)(2,1)S(1)}, bf16[128,1024]{0,1:T(8,128)(2,1)S(1)}, u32[]{:S(2)}, u32[]{:S(2)}) collective-permute-start(bf16[128,1024]{0,1:T(8,128)(2,1)S(1)} %bitcast.262), channel_id=1, source_target_pairs={{0,16},{4,20},{8,24},{12,28},{16,32},{20,36},{24,40},{28,44},{32,4... | collective-permute-start | bytes 786440 | tf_op jit(solution)/shard_map/ppermute | solution.py:35
  637.6 1.5 collective-permute-start.13
  639.3 2.7 collective-permute-done.12
  642.1 4.4 collective-permute-done.13
  646.8 1.4 copy-done.2
  648.2 57.1 %while.31 = (s32[]{:T(128)}, f32[4,128,2,2,128]{1,4,3,2,0:T(8,128)}, f32[4,1152,2,128]{1,3,2,0:T(8,128)}, f32[4,1152,2,128]{1,3,2,0:T(8,128)}, bf16[4,1152,2,128...) while((s32[]{:T(128)}, ...), condition=%wide.region_7.8_spmd.clone, body=%wide.region_5.7_spmd.clone.sunk | while | flops 912131200 | bytes 24730428 | solution.py:158
  650.2 1.9 fusion.96
  652.2 1.5 fusion.97
  653.7 1.6 fusion.98
  655.3 2.1 fusion.99
  657.5 2.4 fusion.101
  659.9 2.5 fusion.100
  664.6 1.9 fusion.96
  666.5 1.5 fusion.97
  668.0 1.6 fusion.98
  669.6 2.1 fusion.99
  671.8 2.4 fusion.101
  674.2 2.5 fusion.100
  678.8 1.9 fusion.96
  680.7 1.5 fusion.97
  682.2 1.6 fusion.98
  683.9 2.1 fusion.99
  686.0 2.5 fusion.101
  688.5 2.5 fusion.100
  693.1 1.9 fusion.96
  695.1 1.5 fusion.97
  696.6 1.6 fusion.98
  698.2 2.1 fusion.99
  700.3 2.4 fusion.101
  702.8 2.5 fusion.100
  706.6 1.4 copy.232
  708.0 4.1 bitcast_convert_fusion.2
  712.1 1.9 slice.144
  713.9 4.1 bitcast_convert_fusion.1
  720.1 1.4 copy.233
  721.5 1.8 multiply_add_fusion.1
  724.5 2.9 fusion.55
  731.2 1.8 fusion.41
  733.0 2.1 reshape.221
  737.7 20.8 %collective-permute-done.23 = bf16[128,1024]{0,1:T(8,128)(2,1)} collective-permute-done((bf16[128,1024]{0,1:T(8,128)(2,1)}, bf16[128,1024]{0,1:T(8,128)(2,1)}, u32[]{:S(2)}, u32[]{:S(2)}) %collective-permute-start.23) | collective-permute-done | bytes 262176 | tf_op jit(solution)/shard_map/ppermute | solution.py:35
  761.1 38.7 %collective-permute-done.22 = bf16[128,1024]{0,1:T(8,128)(2,1)} collective-permute-done((bf16[128,1024]{0,1:T(8,128)(2,1)}, bf16[128,1024]{0,1:T(8,128)(2,1)}, u32[]{:S(2)}, u32[]{:S(2)}) %collective-permute-start.22) | collective-permute-done | bytes 262176 | tf_op jit(solution)/shard_map/ppermute | solution.py:35
  801.1 1.7 fusion.54
  816.2 1.6 fusion.49
  819.3 6.8 collective-permute-done.25
  827.5 4.6 collective-permute-done.26
  836.1 224.7 %all-reduce.7 = (f32[128]{0:T(128)}, f32[128]{0:T(128)}) all-reduce(f32[128]{0:T(128)S(1)} %get-tuple-element.251, f32[128]{0:T(128)S(1)} %get-tuple-element.253), channel_id=1, replica_groups=mesh['seq'=128,'dp'=4] {'seq','dp'}, use_global_device_ids=true, to_apply=%region_11.12 | all-reduce | flops 256 | bytes 2048 | tf_op jit(solution)/shard_map/psum | solution.py:178
  1060.8 2.5 fusion.50
  (504 shorter events, 211.2 us)
Async XLA Ops:
  0.6 15.0 %copy-start.32 = (f32[128]{0:T(128)S(1)}, f32[128]{0:T(128)}, u32[]{:S(2)}) copy-start(f32[128]{0:T(128)} %param.17) | copy-start | bytes 1540
  1.8 644.8 %collective-permute-start.15 = (bf16[128,1024]{0,1:T(8,128)(2,1)S(1)}, bf16[128,1024]{0,1:T(8,128)(2,1)S(1)}, u32[]{:S(2)}, u32[]{:S(2)}) collective-permute-start(bf16[128,1024]{0,1:T(8,128)(2,1)S(1)} %bitcast.256), channel_id=1, source_target_pairs={{0,4},{4,8},{8,12},{12,16},{16,20},{20,24},{24,28},{28,32},{32,36}... | collective-permute-start | bytes 786440 | tf_op jit(solution)/shard_map/ppermute | solution.py:35
  5.8 640.7 %collective-permute-start.14 = (bf16[128,1024]{0,1:T(8,128)(2,1)S(1)}, bf16[128,1024]{0,1:T(8,128)(2,1)S(1)}, u32[]{:S(2)}, u32[]{:S(2)}) collective-permute-start(bf16[128,1024]{0,1:T(8,128)(2,1)S(1)} %bitcast.257), channel_id=1, source_target_pairs={{0,8},{4,12},{8,16},{12,20},{16,24},{20,28},{24,32},{28,36},{32,40... | collective-permute-start | bytes 786440 | tf_op jit(solution)/shard_map/ppermute | solution.py:35
  10.1 549.1 %collective-permute-start.8 = (bf16[128,1024]{0,1:T(8,128)(2,1)S(1)}, bf16[128,1024]{0,1:T(8,128)(2,1)S(1)}, u32[]{:S(2)}, u32[]{:S(2)}) collective-permute-start(bf16[128,1024]{0,1:T(8,128)(2,1)S(1)} %bitcast.258), channel_id=1, source_target_pairs={{0,32},{4,36},{8,40},{12,44},{16,48},{20,52},{24,56},{28,60},{32,6... | collective-permute-start | bytes 786440 | tf_op jit(solution)/shard_map/ppermute | solution.py:35
  15.1 9.2 copy-start.34
  15.1 529.1 %copy-start.16 = (bf16[1,128,2048]{2,1,0:T(8,128)(2,1)S(1)}, bf16[1,128,2048]{2,1,0:T(8,128)(2,1)}, u32[]{:S(2)}) copy-start(bf16[1,128,2048]{2,1,0:T(8,128)(2,1)} %param.11) | copy-start | bytes 1572868
  15.2 529.2 %copy-start.24 = (f32[128,8]{0,1:T(8,128)}, f32[128,8]{0,1:T(8,128)S(1)}, u32[]{:S(2)}) copy-start(f32[128,8]{0,1:T(8,128)S(1)} %copy.167) | copy-start | bytes 12292
  15.3 528.9 %copy-start.14 = (f32[128,8]{1,0:T(8,128)}, f32[128,8]{1,0:T(8,128)S(1)}, u32[]{:S(2)}) copy-start(f32[128,8]{1,0:T(8,128)S(1)} %copy.168) | copy-start | bytes 12292
  15.7 529.8 %copy-start.8 = (f32[128,64]{1,0:T(8,128)}, f32[128,64]{1,0:T(8,128)S(1)}, u32[]{:S(2)}) copy-start(f32[128,64]{1,0:T(8,128)S(1)} %get-tuple-element.321) | copy-start | bytes 98308
  15.7 529.8 %copy-start.10 = (f32[128,64]{1,0:T(8,128)}, f32[128,64]{1,0:T(8,128)S(1)}, u32[]{:S(2)}) copy-start(f32[128,64]{1,0:T(8,128)S(1)} %get-tuple-element.322) | copy-start | bytes 98308
  16.6 544.0 %collective-permute-start.1 = (bf16[128,1024]{0,1:T(8,128)(2,1)S(1)}, bf16[128,1024]{0,1:T(8,128)(2,1)}, u32[]{:S(2)}, u32[]{:S(2)}) collective-permute-start(bf16[128,1024]{0,1:T(8,128)(2,1)S(1)} %bitcast.265), channel_id=1, source_target_pairs={{0,28},{4,32},{8,36},{12,40},{16,44},{20,48},{24,52},{28,56},{32,6... | collective-permute-start | bytes 786440 | tf_op jit(solution)/shard_map/ppermute | solution.py:35
  21.5 526.8 %collective-permute-start = (bf16[128,1024]{0,1:T(8,128)(2,1)S(1)}, bf16[128,1024]{0,1:T(8,128)(2,1)}, u32[]{:S(2)}, u32[]{:S(2)}) collective-permute-start(bf16[128,1024]{0,1:T(8,128)(2,1)S(1)} %bitcast.266), channel_id=1, source_target_pairs={{0,32},{4,36},{8,40},{12,44},{16,48},{20,52},{24,56},{28,60},{32,6... | collective-permute-start | bytes 786440 | tf_op jit(solution)/shard_map/ppermute | solution.py:35
  548.3 21.7 %collective-permute-start.2 = (bf16[128,1024]{0,1:T(8,128)(2,1)S(1)}, bf16[128,1024]{0,1:T(8,128)(2,1)S(1)}, u32[]{:S(2)}, u32[]{:S(2)}) collective-permute-start(bf16[128,1024]{0,1:T(8,128)(2,1)S(1)} %bitcast.267), channel_id=1, source_target_pairs={{0,24},{4,28},{8,32},{12,36},{16,40},{20,44},{24,48},{28,52},{32,5... | collective-permute-start | bytes 786440 | tf_op jit(solution)/shard_map/ppermute | solution.py:35
  559.2 32.9 %collective-permute-start.3 = (bf16[128,1024]{0,1:T(8,128)(2,1)S(1)}, bf16[128,1024]{0,1:T(8,128)(2,1)S(1)}, u32[]{:S(2)}, u32[]{:S(2)}) collective-permute-start(bf16[128,1024]{0,1:T(8,128)(2,1)S(1)} %bitcast.268), channel_id=1, source_target_pairs={{0,20},{4,24},{8,28},{12,32},{16,36},{20,40},{24,44},{28,48},{32,5... | collective-permute-start | bytes 786440 | tf_op jit(solution)/shard_map/ppermute | solution.py:35
  560.5 32.9 %collective-permute-start.4 = (bf16[128,1024]{0,1:T(8,128)(2,1)S(1)}, bf16[128,1024]{0,1:T(8,128)(2,1)S(1)}, u32[]{:S(2)}, u32[]{:S(2)}) collective-permute-start(bf16[128,1024]{0,1:T(8,128)(2,1)S(1)} %bitcast.269), channel_id=1, source_target_pairs={{0,16},{4,20},{8,24},{12,28},{16,32},{20,36},{24,40},{28,44},{32,4... | collective-permute-start | bytes 786440 | tf_op jit(solution)/shard_map/ppermute | solution.py:35
  570.0 24.9 %collective-permute-start.5 = (bf16[128,1024]{0,1:T(8,128)(2,1)S(1)}, bf16[128,1024]{0,1:T(8,128)(2,1)S(1)}, u32[]{:S(2)}, u32[]{:S(2)}) collective-permute-start(bf16[128,1024]{0,1:T(8,128)(2,1)S(1)} %bitcast.270), channel_id=1, source_target_pairs={{0,12},{4,16},{8,20},{12,24},{16,28},{20,32},{24,36},{28,40},{32,4... | collective-permute-start | bytes 786440 | tf_op jit(solution)/shard_map/ppermute | solution.py:35
  592.0 11.4 %collective-permute-start.6 = (bf16[128,1024]{0,1:T(8,128)(2,1)S(1)}, bf16[128,1024]{0,1:T(8,128)(2,1)S(1)}, u32[]{:S(2)}, u32[]{:S(2)}) collective-permute-start(bf16[128,1024]{0,1:T(8,128)(2,1)S(1)} %bitcast.271), channel_id=1, source_target_pairs={{0,8},{4,12},{8,16},{12,20},{16,24},{20,28},{24,32},{28,36},{32,40... | collective-permute-start | bytes 786440 | tf_op jit(solution)/shard_map/ppermute | solution.py:35
  593.4 21.8 %collective-permute-start.7 = (bf16[128,1024]{0,1:T(8,128)(2,1)S(1)}, bf16[128,1024]{0,1:T(8,128)(2,1)S(1)}, u32[]{:S(2)}, u32[]{:S(2)}) collective-permute-start(bf16[128,1024]{0,1:T(8,128)(2,1)S(1)} %bitcast.272), channel_id=1, source_target_pairs={{0,4},{4,8},{8,12},{12,16},{16,20},{20,24},{24,28},{28,32},{32,36}... | collective-permute-start | bytes 786440 | tf_op jit(solution)/shard_map/ppermute | solution.py:35
  594.8 44.4 %collective-permute-start.11 = (bf16[128,1024]{0,1:T(8,128)(2,1)S(1)}, bf16[128,1024]{0,1:T(8,128)(2,1)S(1)}, u32[]{:S(2)}, u32[]{:S(2)}) collective-permute-start(bf16[128,1024]{0,1:T(8,128)(2,1)S(1)} %bitcast.259), channel_id=1, source_target_pairs={{0,20},{4,24},{8,28},{12,32},{16,36},{20,40},{24,44},{28,48},{32,5... | collective-permute-start | bytes 786440 | tf_op jit(solution)/shard_map/ppermute | solution.py:35
  603.4 21.3 %collective-permute-start.9 = (bf16[128,1024]{0,1:T(8,128)(2,1)S(1)}, bf16[128,1024]{0,1:T(8,128)(2,1)S(1)}, u32[]{:S(2)}, u32[]{:S(2)}) collective-permute-start(bf16[128,1024]{0,1:T(8,128)(2,1)S(1)} %bitcast.260), channel_id=1, source_target_pairs={{0,28},{4,32},{8,36},{12,40},{16,44},{20,48},{24,52},{28,56},{32,6... | collective-permute-start | bytes 786440 | tf_op jit(solution)/shard_map/ppermute | solution.py:35
  615.2 22.4 %collective-permute-start.10 = (bf16[128,1024]{0,1:T(8,128)(2,1)S(1)}, bf16[128,1024]{0,1:T(8,128)(2,1)S(1)}, u32[]{:S(2)}, u32[]{:S(2)}) collective-permute-start(bf16[128,1024]{0,1:T(8,128)(2,1)S(1)} %bitcast.261), channel_id=1, source_target_pairs={{0,24},{4,28},{8,32},{12,36},{16,40},{20,44},{24,48},{28,52},{32,5... | collective-permute-start | bytes 786440 | tf_op jit(solution)/shard_map/ppermute | solution.py:35
  624.6 23.5 %copy-start.26 = (s32[128]{0:T(128)S(1)}, s32[128]{0:T(128)}, u32[]{:S(2)}) copy-start(s32[128]{0:T(128)} %compare_select_fusion) | copy-start | bytes 1540
  624.6 23.5 %copy-start.28 = (s32[128]{0:T(128)S(1)}, s32[128]{0:T(128)}, u32[]{:S(2)}) copy-start(s32[128]{0:T(128)} %get-tuple-element.461) | copy-start | bytes 1540
  624.7 22.0 %copy-start.5 = (bf16[1152,4,2,128]{0,3,2,1:T(8,128)(2,1)}, bf16[1152,4,2,128]{0,3,2,1:T(8,128)(2,1)S(1)}, u32[]{:S(2)}) copy-start(bf16[1152,4,2,128]{0,3,2,1:T(8,128)(2,1)S(1)} %constant_dynamic-update-slice_fusion) | copy-start | bytes 7077892
  624.7 17.3 %collective-permute-start.12 = (bf16[128,1024]{0,1:T(8,128)(2,1)S(1)}, bf16[128,1024]{0,1:T(8,128)(2,1)S(1)}, u32[]{:S(2)}, u32[]{:S(2)}) collective-permute-start(bf16[128,1024]{0,1:T(8,128)(2,1)S(1)} %bitcast.262), channel_id=1, source_target_pairs={{0,16},{4,20},{8,24},{12,28},{16,32},{20,36},{24,40},{28,44},{32,4... | collective-permute-start | bytes 786440 | tf_op jit(solution)/shard_map/ppermute | solution.py:35
  637.6 8.8 collective-permute-start.13
  659.9 2.5 copy-start.4
  659.9 2.5 copy-start.19
  659.9 2.5 copy-start.27
  659.9 2.5 copy-start.29
  674.2 2.5 copy-start.4
  674.2 2.5 copy-start.19
  674.2 2.5 copy-start.27
  674.2 2.5 copy-start.29
  688.5 2.5 copy-start.4
  688.5 2.5 copy-start.19
  688.5 2.5 copy-start.27
  688.5 2.5 copy-start.29
  702.8 2.5 copy-start.19
  702.8 2.5 copy-start.27
  702.8 2.5 copy-start.29
  718.0 3.5 copy-start.9
  718.0 3.5 copy-start.11
  727.4 31.2 %collective-permute-start.23 = (bf16[128,1024]{0,1:T(8,128)(2,1)}, bf16[128,1024]{0,1:T(8,128)(2,1)}, u32[]{:S(2)}, u32[]{:S(2)}) collective-permute-start(bf16[128,1024]{0,1:T(8,128)(2,1)} %bitcast.46), channel_id=1, source_target_pairs={{32,0},{36,4},{40,8},{44,12},{48,16},{52,20},{56,24},{60,28},{64,3... | collective-permute-start | bytes 786440 | tf_op jit(solution)/shard_map/ppermute | solution.py:35
  728.6 31.2 %collective-permute-start.16 = (bf16[128,1024]{0,1:T(8,128)(2,1)}, bf16[128,1024]{0,1:T(8,128)(2,1)}, u32[]{:S(2)}, u32[]{:S(2)}) collective-permute-start(bf16[128,1024]{0,1:T(8,128)(2,1)} %bitcast.39), channel_id=1, source_target_pairs={{4,0},{8,4},{12,8},{16,12},{20,16},{24,20},{28,24},{32,28},{36,32}... | collective-permute-start | bytes 786440 | tf_op jit(solution)/shard_map/ppermute | solution.py:35
  729.9 69.9 %collective-permute-start.22 = (bf16[128,1024]{0,1:T(8,128)(2,1)}, bf16[128,1024]{0,1:T(8,128)(2,1)}, u32[]{:S(2)}, u32[]{:S(2)}) collective-permute-start(bf16[128,1024]{0,1:T(8,128)(2,1)} %bitcast.45), channel_id=1, source_target_pairs={{28,0},{32,4},{36,8},{40,12},{44,16},{48,20},{52,24},{56,28},{60,3... | collective-permute-start | bytes 786440 | tf_op jit(solution)/shard_map/ppermute | solution.py:35
  735.1 74.6 %collective-permute-start.21 = (bf16[128,1024]{0,1:T(8,128)(2,1)}, bf16[128,1024]{0,1:T(8,128)(2,1)S(1)}, u32[]{:S(2)}, u32[]{:S(2)}) collective-permute-start(bf16[128,1024]{0,1:T(8,128)(2,1)} %bitcast.278), channel_id=1, source_target_pairs={{24,0},{28,4},{32,8},{36,12},{40,16},{44,20},{48,24},{52,28},{56,3... | collective-permute-start | bytes 786440 | tf_op jit(solution)/shard_map/ppermute | solution.py:35
  736.4 74.6 %collective-permute-start.20 = (bf16[128,1024]{0,1:T(8,128)(2,1)}, bf16[128,1024]{0,1:T(8,128)(2,1)S(1)}, u32[]{:S(2)}, u32[]{:S(2)}) collective-permute-start(bf16[128,1024]{0,1:T(8,128)(2,1)} %bitcast.277), channel_id=1, source_target_pairs={{20,0},{24,4},{28,8},{32,12},{36,16},{40,20},{44,24},{48,28},{52,3... | collective-permute-start | bytes 786440 | tf_op jit(solution)/shard_map/ppermute | solution.py:35
  758.5 53.7 %collective-permute-start.19 = (bf16[128,1024]{0,1:T(8,128)(2,1)}, bf16[128,1024]{0,1:T(8,128)(2,1)S(1)}, u32[]{:S(2)}, u32[]{:S(2)}) collective-permute-start(bf16[128,1024]{0,1:T(8,128)(2,1)} %bitcast.276), channel_id=1, source_target_pairs={{16,0},{20,4},{24,8},{28,12},{32,16},{36,20},{40,24},{44,28},{48,3... | collective-permute-start | bytes 786440 | tf_op jit(solution)/shard_map/ppermute | solution.py:35
  759.8 53.7 %collective-permute-start.18 = (bf16[128,1024]{0,1:T(8,128)(2,1)}, bf16[128,1024]{0,1:T(8,128)(2,1)}, u32[]{:S(2)}, u32[]{:S(2)}) collective-permute-start(bf16[128,1024]{0,1:T(8,128)(2,1)} %bitcast.275), channel_id=1, source_target_pairs={{12,0},{16,4},{20,8},{24,12},{28,16},{32,20},{36,24},{40,28},{44,3... | collective-permute-start | bytes 786440 | tf_op jit(solution)/shard_map/ppermute | solution.py:35
  799.8 15.1 %collective-permute-start.17 = (bf16[128,1024]{0,1:T(8,128)(2,1)}, bf16[128,1024]{0,1:T(8,128)(2,1)}, u32[]{:S(2)}, u32[]{:S(2)}) collective-permute-start(bf16[128,1024]{0,1:T(8,128)(2,1)} %bitcast.274), channel_id=1, source_target_pairs={{8,0},{12,4},{16,8},{20,12},{24,16},{28,20},{32,24},{36,28},{40,32... | collective-permute-start | bytes 786440 | tf_op jit(solution)/shard_map/ppermute | solution.py:35
  802.8 13.4 %copy-start.7 = (f32[128,4,2,128]{0,3,2,1:T(8,128)S(1)}, f32[128,4,2,128]{0,3,2,1:T(8,128)}, u32[]{:S(2)}) copy-start(f32[128,4,2,128]{0,3,2,1:T(8,128)} %slice.144) | copy-start | bytes 1572868
  809.6 16.5 %collective-permute-start.25 = (bf16[128,1024]{1,0:T(8,128)(2,1)}, bf16[128,1024]{1,0:T(8,128)(2,1)}, u32[]{:S(2)}, u32[]{:S(2)}) collective-permute-start(bf16[128,1024]{1,0:T(8,128)(2,1)} %copy.218), channel_id=1, source_target_pairs={{8,0},{12,4},{16,8},{20,12},{24,16},{28,20},{32,24},{36,28},{40,32... | collective-permute-start | bytes 786440 | tf_op jit(solution)/shard_map/ppermute | solution.py:35
  810.9 21.1 %collective-permute-start.26 = (bf16[128,1024]{1,0:T(8,128)(2,1)}, bf16[128,1024]{1,0:T(8,128)(2,1)}, u32[]{:S(2)}, u32[]{:S(2)}) collective-permute-start(bf16[128,1024]{1,0:T(8,128)(2,1)} %copy.219), channel_id=1, source_target_pairs={{12,0},{16,4},{20,8},{24,12},{28,16},{32,20},{36,24},{40,28},{44,3... | collective-permute-start | bytes 786440 | tf_op jit(solution)/shard_map/ppermute | solution.py:35
  812.2 21.1 %collective-permute-start.27 = (bf16[128,1024]{1,0:T(8,128)(2,1)}, bf16[128,1024]{1,0:T(8,128)(2,1)}, u32[]{:S(2)}, u32[]{:S(2)}) collective-permute-start(bf16[128,1024]{1,0:T(8,128)(2,1)} %copy.220), channel_id=1, source_target_pairs={{16,0},{20,4},{24,8},{28,12},{32,16},{36,20},{40,24},{44,28},{48,3... | collective-permute-start | bytes 786440 | tf_op jit(solution)/shard_map/ppermute | solution.py:35
  813.6 247.2 %collective-permute-start.28 = (bf16[128,1024]{1,0:T(8,128)(2,1)}, bf16[128,1024]{1,0:T(8,128)(2,1)}, u32[]{:S(2)}, u32[]{:S(2)}) collective-permute-start(bf16[128,1024]{1,0:T(8,128)(2,1)} %copy.221), channel_id=1, source_target_pairs={{20,0},{24,4},{28,8},{32,12},{36,16},{40,20},{44,24},{48,28},{52,3... | collective-permute-start | bytes 786440 | tf_op jit(solution)/shard_map/ppermute | solution.py:35
  814.9 245.9 %collective-permute-start.29 = (bf16[128,1024]{1,0:T(8,128)(2,1)}, bf16[128,1024]{1,0:T(8,128)(2,1)}, u32[]{:S(2)}, u32[]{:S(2)}) collective-permute-start(bf16[128,1024]{1,0:T(8,128)(2,1)} %copy.222), channel_id=1, source_target_pairs={{24,0},{28,4},{32,8},{36,12},{40,16},{44,20},{48,24},{52,28},{56,3... | collective-permute-start | bytes 786440 | tf_op jit(solution)/shard_map/ppermute | solution.py:35
  818.3 13.7 %copy-start.21 = (bf16[128,1024]{1,0:T(8,128)(2,1)S(1)}, bf16[128,1024]{1,0:T(8,128)(2,1)}, u32[]{:S(2)}) copy-start(bf16[128,1024]{1,0:T(8,128)(2,1)} %copy.224) | copy-start | bytes 786436
  818.3 15.0 %copy-start.20 = (bf16[128,1024]{1,0:T(8,128)(2,1)S(1)}, bf16[128,1024]{1,0:T(8,128)(2,1)}, u32[]{:S(2)}) copy-start(bf16[128,1024]{1,0:T(8,128)(2,1)} %copy.217) | copy-start | bytes 786436
  818.3 16.3 %copy-start.25 = (f32[128,8]{0,1:T(8,128)S(1)}, f32[128,8]{0,1:T(8,128)}, u32[]{:S(2)}) copy-start(f32[128,8]{0,1:T(8,128)} %copy-done.24) | copy-start | bytes 12292
  818.8 242.0 %copy-start.6 = (f32[128,1024]{1,0:T(8,128)S(1)}, f32[128,1024]{1,0:T(8,128)}, u32[]{:S(2)}) copy-start(f32[128,1024]{1,0:T(8,128)} %copy.216) | copy-start | bytes 1572868
  826.2 234.6 %collective-permute-start.30 = (bf16[128,1024]{1,0:T(8,128)(2,1)}, bf16[128,1024]{1,0:T(8,128)(2,1)S(1)}, u32[]{:S(2)}, u32[]{:S(2)}) collective-permute-start(bf16[128,1024]{1,0:T(8,128)(2,1)} %copy.223), channel_id=1, source_target_pairs={{28,0},{32,4},{36,8},{40,12},{44,16},{48,20},{52,24},{56,28},{60,3... | collective-permute-start | bytes 786440 | tf_op jit(solution)/shard_map/ppermute | solution.py:35
  832.0 228.8 %collective-permute-start.31 = (bf16[128,1024]{1,0:T(8,128)(2,1)S(1)}, bf16[128,1024]{1,0:T(8,128)(2,1)}, u32[]{:S(2)}, u32[]{:S(2)}) collective-permute-start(bf16[128,1024]{1,0:T(8,128)(2,1)S(1)} %copy-done.21), channel_id=1, source_target_pairs={{32,0},{36,4},{40,8},{44,12},{48,16},{52,20},{56,24},{60,28},{64,3... | collective-permute-start | bytes 786440 | tf_op jit(solution)/shard_map/ppermute | solution.py:35
  833.3 227.5 %collective-permute-start.24 = (bf16[128,1024]{1,0:T(8,128)(2,1)S(1)}, bf16[128,1024]{1,0:T(8,128)(2,1)}, u32[]{:S(2)}, u32[]{:S(2)}) collective-permute-start(bf16[128,1024]{1,0:T(8,128)(2,1)S(1)} %copy-done.20), channel_id=1, source_target_pairs={{4,0},{8,4},{12,8},{16,12},{20,16},{24,20},{28,24},{32,28},{36,32}... | collective-permute-start | bytes 786440 | tf_op jit(solution)/shard_map/ppermute | solution.py:35
  (21 other events, 28.7 us)
where the time goes:
time: 1080 us; the launch traced here: 1060 us
  loops' own time  337 us (31%)
  blocking collectives  253 us (23%)
  local copies, waits for them, and re-layouts  192 us (18%)
  waiting for transfers between devices  107 us (10%)
  starting transfers between devices  99.1 us (9%)
  matrix products  48.5 us (4%)
  other arithmetic  24.7 us (2%)
    another operation x1, loops' own time, entering(): return lax.fori_loop(0, length, turn, start)  337 us
    psum x1, blocking collectives, shards(): lax.psum((query_gain_gradient, key_gain_gradient), ('seq', 'dp'))  225 us
    dynamic_slice x256, local copies, waits for them, and re-layouts, turn(): new = combine(before, jax.tree.map(lambda part: part[k], everything))  150 us
    ppermute x32, waiting for transfers between devices, from_behind(): lax.ppermute(value, axis, [(source, source + steps) for source in range(f...  107 us
    ppermute x32, starting transfers between devices, from_behind(): lax.ppermute(value, axis, [(source, source + steps) for source in range(f...  99.1 us
    all_gather x1, blocking collectives, entering(): everything = jax.tree.map(lambda part: lax.all_gather(part, axis), value)  28.4 us
  transfers between devices with their start and end apart: 32, of which 9 were waited for; matrix products, arithmetic and copies ran while one was open for 17% of the time, Pallas kernels for 0%

commit v1 on v0

--- a/solution.py
+++ b/solution.py
@@ -2,6 +2,7 @@
 import jax.numpy as jnp
 from jax import lax
 from jax.sharding import PartitionSpec as P
+from jax.lax import psum
 
 HEAD_SIZE = 128
 QUERY_HEADS = 16
@@ -175,7 +176,7 @@
     key_raw_gradient, key_gain_gradient = key_backward(
         key_full_length.reshape(row_count, KEY_VALUE_HEADS, HEAD_SIZE)
     )
-    gain_query, gain_key = lax.psum((query_gain_gradient, key_gain_gradient), ("seq", "dp"))
+    gain_query, gain_key = psum(psum((query_gain_gradient, key_gain_gradient), "seq"), "dp")
     return (
         query_raw_gradient.astype(jnp.bfloat16).reshape(1, row_count, QUERY_HEADS * HEAD_SIZE),
         key_raw_gradient.astype(jnp.bfloat16).reshape(1, row_count, key_span_width),

time: 1080 us -> 1340 us (1.24)
  the two profiles are of different devices: /device:TPU:1 before, /device:TPU:264 now
where the time goes in v1:
time: 1340 us; the launch traced here: 1330 us
  blocking collectives  415 us (31%)
  loops' own time  337 us (25%)
  local copies, waits for them, and re-layouts  192 us (14%)
  starting transfers between devices  182 us (14%)
  waiting for transfers between devices  124 us (9%)
  matrix products  48.5 us (4%)
  other arithmetic  24.6 us (2%)
    psum x1, blocking collectives, shards(): psum((query_gain_gradient, key_gain_gradient), 'seq')  381 us
    another operation x1, loops' own time, entering(): return lax.fori_loop(0, length, turn, start)  337 us
    ppermute x32, starting transfers between devices, from_behind(): lax.ppermute(value, axis, [(source, source + steps) for source in range(f...  182 us
    dynamic_slice x256, local copies, waits for them, and re-layouts, turn(): new = combine(before, jax.tree.map(lambda part: part[k], everything))  150 us
    ppermute x32, waiting for transfers between devices, from_behind(): lax.ppermute(value, axis, [(source, source + steps) for source in range(f...  124 us
    all_gather x1, blocking collectives, entering(): everything = jax.tree.map(lambda part: lax.all_gather(part, axis), value)  27.8 us
  transfers between devices with their start and end apart: 32, of which 12 were waited for; matrix products, arithmetic and copies ran while one was open for 14% of the time, Pallas kernels for 0%

profile of v1, /device:TPU:264, one launch (start us, length us, event | category | flops | bytes accessed | tf_op | source)
XLA Modules:
  0.0 1325.1 jit_solution(6588641132423515834)
XLA Ops:
  1.8 3.5 collective-permute-start.15
  5.3 5.7 collective-permute-start.14
  11.0 3.4 collective-permute-start.8
  17.7 2.1 collective-permute-start.1
  19.8 3.2 collective-permute-start
  27.2 27.8 %all-reduce.6 = (s32[128]{0:T(128)S(1)}, s32[128]{0:T(128)S(1)}) all-reduce(s32[128]{0:T(128)S(1)} %bitcast_dynamic-update-slice_fusion, s32[128]{0:T(128)S(1)} %slice_dynamic-update-slice_fusion), channel_id=2, replica_groups=mesh['seq'=128,'dp'=4] {'seq'}, use_global_device_ids=true, to_apply=%add.4 | all-reduce | flops 256 | bytes 2048 | tf_op jit(solution)/shard_map/all_gather | solution.py:18
  55.0 487.3 %while.30 = (s32[]{:T(128)}, s32[]{:T(128)}, s32[]{:T(128)}, s32[]{:T(128)}, s32[128]{0:T(128)S(1)}, /*index=5*/s32[128]{0:T(128)S(1)}, s32[]{:T(128)}, s32[]{:T(128)}) while((s32[]{:T(128)}, s32[]{:T(128)}, s32[]{:T(128)}, s32[]{:T(128)}, s32[128]{0:T(128)S(1)}, /*index=5*/s32[128]{0:T(128)S(1)}, s32[]{:T(128)}, s32[]{:T(128)}) %tuple.77), condition=%wide.region_4.5_spmd, body=%wide.region_3.4_spmd.sunk | while | flops 10 | bytes 199 | solution.py:30
  546.2 3.9 collective-permute-start.2
  551.2 11.3 collective-permute-start.3
  562.6 1.9 collective-permute-start.4
  565.5 4.9 collective-permute-done.2
  570.4 13.5 %collective-permute-start.5 = (bf16[128,1024]{0,1:T(8,128)(2,1)S(1)}, bf16[128,1024]{0,1:T(8,128)(2,1)S(1)}, u32[]{:S(2)}, u32[]{:S(2)}) collective-permute-start(bf16[128,1024]{0,1:T(8,128)(2,1)S(1)} %bitcast.270), channel_id=1, source_target_pairs={{0,12},{4,16},{8,20},{12,24},{16,28},{20,32},{24,36},{28,40},{32,4... | collective-permute-start | bytes 786440 | tf_op jit(solution)/shard_map/ppermute | solution.py:36
  584.9 8.5 collective-permute-start.6
  593.4 9.8 collective-permute-done.4
  603.2 3.1 collective-permute-start.7
  606.3 6.2 collective-permute-done.5
  614.6 8.2 collective-permute-done.6
  624.7 1.9 collective-permute-start.10
  626.8 34.6 %collective-permute-done.9 = bf16[128,1024]{0,1:T(8,128)(2,1)S(1)} collective-permute-done((bf16[128,1024]{0,1:T(8,128)(2,1)S(1)}, bf16[128,1024]{0,1:T(8,128)(2,1)S(1)}, u32[]{:S(2)}, u32[]{:S(2)}) %collective-permute-start.9) | collective-permute-done | bytes 262176 | tf_op jit(solution)/shard_map/ppermute | solution.py:36
  663.4 2.1 collective-permute-start.13
  665.7 19.1 %collective-permute-done.12 = bf16[128,1024]{0,1:T(8,128)(2,1)S(1)} collective-permute-done((bf16[128,1024]{0,1:T(8,128)(2,1)S(1)}, bf16[128,1024]{0,1:T(8,128)(2,1)S(1)}, u32[]{:S(2)}, u32[]{:S(2)}) %collective-permute-start.12) | collective-permute-done | bytes 262176 | tf_op jit(solution)/shard_map/ppermute | solution.py:36
  684.9 6.3 collective-permute-done.13
  692.9 57.1 %while.31 = (s32[]{:T(128)}, f32[4,128,2,2,128]{1,4,3,2,0:T(8,128)}, f32[4,1152,2,128]{1,3,2,0:T(8,128)}, f32[4,1152,2,128]{1,3,2,0:T(8,128)}, bf16[4,1152,2,128...) while((s32[]{:T(128)}, ...), condition=%wide.region_7.8_spmd.clone, body=%wide.region_5.7_spmd.clone.sunk | while | flops 912131200 | bytes 24730428 | solution.py:159
  695.0 1.9 fusion.96
  700.1 2.2 fusion.99
  702.3 2.4 fusion.101
  704.7 2.5 fusion.100
  709.3 1.9 fusion.96
  714.4 2.2 fusion.99
  716.5 2.4 fusion.101
  718.9 2.5 fusion.100
  723.6 1.9 fusion.96
  728.6 2.1 fusion.99
  730.8 2.5 fusion.101
  733.3 2.5 fusion.100
  737.9 1.9 fusion.96
  743.0 2.1 fusion.99
  745.1 2.4 fusion.101
  747.6 2.5 fusion.100
  752.8 4.1 bitcast_convert_fusion.2
  758.7 4.1 bitcast_convert_fusion.1
  769.3 2.9 fusion.55
  772.2 1.9 collective-permute-start.23
  774.1 9.7 collective-permute-start.16
  783.8 1.9 collective-permute-start.22
  787.5 2.1 reshape.221
  791.5 1.9 collective-permute-start.20
  793.4 44.9 %collective-permute-start.19 = (bf16[128,1024]{0,1:T(8,128)(2,1)}, bf16[128,1024]{0,1:T(8,128)(2,1)S(1)}, u32[]{:S(2)}, u32[]{:S(2)}) collective-permute-start(bf16[128,1024]{0,1:T(8,128)(2,1)} %bitcast.276), channel_id=1, source_target_pairs={{16,0},{20,4},{24,8},{28,12},{32,16},{36,20},{40,24},{44,28},{48,3... | collective-permute-start | bytes 786440 | tf_op jit(solution)/shard_map/ppermute | solution.py:36
  838.4 1.9 collective-permute-start.18
  840.3 15.0 %collective-permute-start.17 = (bf16[128,1024]{0,1:T(8,128)(2,1)}, bf16[128,1024]{0,1:T(8,128)(2,1)}, u32[]{:S(2)}, u32[]{:S(2)}) collective-permute-start(bf16[128,1024]{0,1:T(8,128)(2,1)} %bitcast.274), channel_id=1, source_target_pairs={{8,0},{12,4},{16,8},{20,12},{24,16},{28,20},{32,24},{36,28},{40,32... | collective-permute-start | bytes 786440 | tf_op jit(solution)/shard_map/ppermute | solution.py:36
  863.9 1.9 collective-permute-start.25
  865.8 1.9 collective-permute-start.26
  867.7 1.9 collective-permute-start.27
  869.7 10.8 collective-permute-start.28
  880.5 10.8 collective-permute-done.17
  891.3 1.9 collective-permute-start.29
  896.4 18.3 %collective-permute-done.25 = bf16[128,1024]{1,0:T(8,128)(2,1)} collective-permute-done((bf16[128,1024]{1,0:T(8,128)(2,1)}, bf16[128,1024]{1,0:T(8,128)(2,1)}, u32[]{:S(2)}, u32[]{:S(2)}) %collective-permute-start.25) | collective-permute-done | bytes 262176 | tf_op jit(solution)/shard_map/ppermute | solution.py:36
  916.5 2.6 collective-permute-done.26
  919.2 1.9 collective-permute-start.31
  921.1 2.5 collective-permute-done.27
  923.6 10.4 collective-permute-start.24
  935.5 380.9 %all-reduce.7 = (f32[128]{0:T(128)S(1)}, f32[128]{0:T(128)S(1)}) all-reduce(f32[128]{0:T(128)S(1)} %get-tuple-element.251, f32[128]{0:T(128)S(1)} %get-tuple-element.253), channel_id=1, replica_groups=mesh['seq'=128,'dp'=4] {'seq'}, use_global_device_ids=true, to_apply=%region_11.12 | all-reduce | flops 256 | bytes 2048 | tf_op jit(solution)/shard_map/psum | solution.py:179
  1316.3 6.2 all-reduce.8
  1322.6 2.5 fusion.50
  (505 shorter events, 224.1 us)
Async XLA Ops:
  0.6 16.1 %copy-start.32 = (f32[128]{0:T(128)S(1)}, f32[128]{0:T(128)}, u32[]{:S(2)}) copy-start(f32[128]{0:T(128)} %param.17) | copy-start | bytes 1540
  1.8 689.6 %collective-permute-start.15 = (bf16[128,1024]{0,1:T(8,128)(2,1)S(1)}, bf16[128,1024]{0,1:T(8,128)(2,1)S(1)}, u32[]{:S(2)}, u32[]{:S(2)}) collective-permute-start(bf16[128,1024]{0,1:T(8,128)(2,1)S(1)} %bitcast.256), channel_id=1, source_target_pairs={{0,4},{4,8},{8,12},{12,16},{16,20},{20,24},{24,28},{28,32},{32,36}... | collective-permute-start | bytes 786440 | tf_op jit(solution)/shard_map/ppermute | solution.py:36
  5.3 686.0 %collective-permute-start.14 = (bf16[128,1024]{0,1:T(8,128)(2,1)S(1)}, bf16[128,1024]{0,1:T(8,128)(2,1)S(1)}, u32[]{:S(2)}, u32[]{:S(2)}) collective-permute-start(bf16[128,1024]{0,1:T(8,128)(2,1)S(1)} %bitcast.257), channel_id=1, source_target_pairs={{0,8},{4,12},{8,16},{12,20},{16,24},{20,28},{24,32},{28,36},{32,40... | collective-permute-start | bytes 786440 | tf_op jit(solution)/shard_map/ppermute | solution.py:36
  11.0 540.2 %collective-permute-start.8 = (bf16[128,1024]{0,1:T(8,128)(2,1)S(1)}, bf16[128,1024]{0,1:T(8,128)(2,1)S(1)}, u32[]{:S(2)}, u32[]{:S(2)}) collective-permute-start(bf16[128,1024]{0,1:T(8,128)(2,1)S(1)} %bitcast.258), channel_id=1, source_target_pairs={{0,32},{4,36},{8,40},{12,44},{16,48},{20,52},{24,56},{28,60},{32,6... | collective-permute-start | bytes 786440 | tf_op jit(solution)/shard_map/ppermute | solution.py:36
  16.2 6.8 copy-start.34
  16.3 526.0 %copy-start.16 = (bf16[1,128,2048]{2,1,0:T(8,128)(2,1)S(1)}, bf16[1,128,2048]{2,1,0:T(8,128)(2,1)}, u32[]{:S(2)}) copy-start(bf16[1,128,2048]{2,1,0:T(8,128)(2,1)} %param.11) | copy-start | bytes 1572868
  16.3 526.0 %copy-start.24 = (f32[128,8]{0,1:T(8,128)}, f32[128,8]{0,1:T(8,128)S(1)}, u32[]{:S(2)}) copy-start(f32[128,8]{0,1:T(8,128)S(1)} %copy.167) | copy-start | bytes 12292
  16.4 525.8 %copy-start.14 = (f32[128,8]{1,0:T(8,128)}, f32[128,8]{1,0:T(8,128)S(1)}, u32[]{:S(2)}) copy-start(f32[128,8]{1,0:T(8,128)S(1)} %copy.168) | copy-start | bytes 12292
  16.8 526.7 %copy-start.8 = (f32[128,64]{1,0:T(8,128)}, f32[128,64]{1,0:T(8,128)S(1)}, u32[]{:S(2)}) copy-start(f32[128,64]{1,0:T(8,128)S(1)} %get-tuple-element.323) | copy-start | bytes 98308
  16.8 526.7 %copy-start.10 = (f32[128,64]{1,0:T(8,128)}, f32[128,64]{1,0:T(8,128)S(1)}, u32[]{:S(2)}) copy-start(f32[128,64]{1,0:T(8,128)S(1)} %get-tuple-element.324) | copy-start | bytes 98308
  17.7 544.9 %collective-permute-start.1 = (bf16[128,1024]{0,1:T(8,128)(2,1)S(1)}, bf16[128,1024]{0,1:T(8,128)(2,1)}, u32[]{:S(2)}, u32[]{:S(2)}) collective-permute-start(bf16[128,1024]{0,1:T(8,128)(2,1)S(1)} %bitcast.265), channel_id=1, source_target_pairs={{0,28},{4,32},{8,36},{12,40},{16,44},{20,48},{24,52},{28,56},{32,6... | collective-permute-start | bytes 786440 | tf_op jit(solution)/shard_map/ppermute | solution.py:36
  19.8 526.5 %collective-permute-start = (bf16[128,1024]{0,1:T(8,128)(2,1)S(1)}, bf16[128,1024]{0,1:T(8,128)(2,1)}, u32[]{:S(2)}, u32[]{:S(2)}) collective-permute-start(bf16[128,1024]{0,1:T(8,128)(2,1)S(1)} %bitcast.266), channel_id=1, source_target_pairs={{0,32},{4,36},{8,40},{12,44},{16,48},{20,52},{24,56},{28,60},{32,6... | collective-permute-start | bytes 786440 | tf_op jit(solution)/shard_map/ppermute | solution.py:36
  546.2 24.2 %collective-permute-start.2 = (bf16[128,1024]{0,1:T(8,128)(2,1)S(1)}, bf16[128,1024]{0,1:T(8,128)(2,1)S(1)}, u32[]{:S(2)}, u32[]{:S(2)}) collective-permute-start(bf16[128,1024]{0,1:T(8,128)(2,1)S(1)} %bitcast.267), channel_id=1, source_target_pairs={{0,24},{4,28},{8,32},{12,36},{16,40},{20,44},{24,48},{28,52},{32,5... | collective-permute-start | bytes 786440 | tf_op jit(solution)/shard_map/ppermute | solution.py:36
  551.2 33.7 %collective-permute-start.3 = (bf16[128,1024]{0,1:T(8,128)(2,1)S(1)}, bf16[128,1024]{0,1:T(8,128)(2,1)S(1)}, u32[]{:S(2)}, u32[]{:S(2)}) collective-permute-start(bf16[128,1024]{0,1:T(8,128)(2,1)S(1)} %bitcast.268), channel_id=1, source_target_pairs={{0,20},{4,24},{8,28},{12,32},{16,36},{20,40},{24,44},{28,48},{32,5... | collective-permute-start | bytes 786440 | tf_op jit(solution)/shard_map/ppermute | solution.py:36
  562.6 40.6 %collective-permute-start.4 = (bf16[128,1024]{0,1:T(8,128)(2,1)S(1)}, bf16[128,1024]{0,1:T(8,128)(2,1)S(1)}, u32[]{:S(2)}, u32[]{:S(2)}) collective-permute-start(bf16[128,1024]{0,1:T(8,128)(2,1)S(1)} %bitcast.269), channel_id=1, source_target_pairs={{0,16},{4,20},{8,24},{12,28},{16,32},{20,36},{24,40},{28,44},{32,4... | collective-permute-start | bytes 786440 | tf_op jit(solution)/shard_map/ppermute | solution.py:36
  570.4 42.2 %collective-permute-start.5 = (bf16[128,1024]{0,1:T(8,128)(2,1)S(1)}, bf16[128,1024]{0,1:T(8,128)(2,1)S(1)}, u32[]{:S(2)}, u32[]{:S(2)}) collective-permute-start(bf16[128,1024]{0,1:T(8,128)(2,1)S(1)} %bitcast.270), channel_id=1, source_target_pairs={{0,12},{4,16},{8,20},{12,24},{16,28},{20,32},{24,36},{28,40},{32,4... | collective-permute-start | bytes 786440 | tf_op jit(solution)/shard_map/ppermute | solution.py:36
  584.9 37.9 %collective-permute-start.6 = (bf16[128,1024]{0,1:T(8,128)(2,1)S(1)}, bf16[128,1024]{0,1:T(8,128)(2,1)S(1)}, u32[]{:S(2)}, u32[]{:S(2)}) collective-permute-start(bf16[128,1024]{0,1:T(8,128)(2,1)S(1)} %bitcast.271), channel_id=1, source_target_pairs={{0,8},{4,12},{8,16},{12,20},{16,24},{20,28},{24,32},{28,36},{32,40... | collective-permute-start | bytes 786440 | tf_op jit(solution)/shard_map/ppermute | solution.py:36
  603.2 21.5 %collective-permute-start.7 = (bf16[128,1024]{0,1:T(8,128)(2,1)S(1)}, bf16[128,1024]{0,1:T(8,128)(2,1)S(1)}, u32[]{:S(2)}, u32[]{:S(2)}) collective-permute-start(bf16[128,1024]{0,1:T(8,128)(2,1)S(1)} %bitcast.272), channel_id=1, source_target_pairs={{0,4},{4,8},{8,12},{12,16},{16,20},{20,24},{24,28},{28,32},{32,36}... | collective-permute-start | bytes 786440 | tf_op jit(solution)/shard_map/ppermute | solution.py:36
  612.6 53.0 %collective-permute-start.11 = (bf16[128,1024]{0,1:T(8,128)(2,1)S(1)}, bf16[128,1024]{0,1:T(8,128)(2,1)S(1)}, u32[]{:S(2)}, u32[]{:S(2)}) collective-permute-start(bf16[128,1024]{0,1:T(8,128)(2,1)S(1)} %bitcast.259), channel_id=1, source_target_pairs={{0,20},{4,24},{8,28},{12,32},{16,36},{20,40},{24,44},{28,48},{32,5... | collective-permute-start | bytes 786440 | tf_op jit(solution)/shard_map/ppermute | solution.py:36
  622.7 38.7 %collective-permute-start.9 = (bf16[128,1024]{0,1:T(8,128)(2,1)S(1)}, bf16[128,1024]{0,1:T(8,128)(2,1)S(1)}, u32[]{:S(2)}, u32[]{:S(2)}) collective-permute-start(bf16[128,1024]{0,1:T(8,128)(2,1)S(1)} %bitcast.260), channel_id=1, source_target_pairs={{0,28},{4,32},{8,36},{12,40},{16,44},{20,48},{24,52},{28,56},{32,6... | collective-permute-start | bytes 786440 | tf_op jit(solution)/shard_map/ppermute | solution.py:36
  624.7 38.7 %collective-permute-start.10 = (bf16[128,1024]{0,1:T(8,128)(2,1)S(1)}, bf16[128,1024]{0,1:T(8,128)(2,1)S(1)}, u32[]{:S(2)}, u32[]{:S(2)}) collective-permute-start(bf16[128,1024]{0,1:T(8,128)(2,1)S(1)} %bitcast.261), channel_id=1, source_target_pairs={{0,24},{4,28},{8,32},{12,36},{16,40},{20,44},{24,48},{28,52},{32,5... | collective-permute-start | bytes 786440 | tf_op jit(solution)/shard_map/ppermute | solution.py:36
  626.7 66.2 %copy-start.26 = (s32[128]{0:T(128)S(1)}, s32[128]{0:T(128)}, u32[]{:S(2)}) copy-start(s32[128]{0:T(128)} %compare_select_fusion) | copy-start | bytes 1540
  626.7 66.2 %copy-start.28 = (s32[128]{0:T(128)S(1)}, s32[128]{0:T(128)}, u32[]{:S(2)}) copy-start(s32[128]{0:T(128)} %get-tuple-element.463) | copy-start | bytes 1540
  626.8 64.7 %copy-start.5 = (bf16[1152,4,2,128]{0,3,2,1:T(8,128)(2,1)}, bf16[1152,4,2,128]{0,3,2,1:T(8,128)(2,1)S(1)}, u32[]{:S(2)}) copy-start(bf16[1152,4,2,128]{0,3,2,1:T(8,128)(2,1)S(1)} %constant_dynamic-update-slice_fusion) | copy-start | bytes 7077892
  661.4 23.3 %collective-permute-start.12 = (bf16[128,1024]{0,1:T(8,128)(2,1)S(1)}, bf16[128,1024]{0,1:T(8,128)(2,1)S(1)}, u32[]{:S(2)}, u32[]{:S(2)}) collective-permute-start(bf16[128,1024]{0,1:T(8,128)(2,1)S(1)} %bitcast.262), channel_id=1, source_target_pairs={{0,16},{4,20},{8,24},{12,28},{16,32},{20,36},{24,40},{28,44},{32,4... | collective-permute-start | bytes 786440 | tf_op jit(solution)/shard_map/ppermute | solution.py:36
  663.4 27.7 %collective-permute-start.13 = (bf16[128,1024]{0,1:T(8,128)(2,1)S(1)}, bf16[128,1024]{0,1:T(8,128)(2,1)S(1)}, u32[]{:S(2)}, u32[]{:S(2)}) collective-permute-start(bf16[128,1024]{0,1:T(8,128)(2,1)S(1)} %bitcast.263), channel_id=1, source_target_pairs={{0,12},{4,16},{8,20},{12,24},{16,28},{20,32},{24,36},{28,40},{32,4... | collective-permute-start | bytes 786440 | tf_op jit(solution)/shard_map/ppermute | solution.py:36
  704.7 2.5 copy-start.4
  704.7 2.5 copy-start.19
  704.7 2.5 copy-start.27
  704.7 2.5 copy-start.29
  718.9 2.5 copy-start.4
  718.9 2.5 copy-start.19
  718.9 2.5 copy-start.27
  718.9 2.5 copy-start.29
  733.3 2.5 copy-start.19
  733.3 2.5 copy-start.27
  733.3 2.5 copy-start.29
  747.5 2.5 copy-start.4
  747.5 2.5 copy-start.19
  747.6 2.5 copy-start.27
  747.6 2.5 copy-start.29
  762.8 3.5 copy-start.9
  762.8 3.5 copy-start.11
  772.2 21.3 %collective-permute-start.23 = (bf16[128,1024]{0,1:T(8,128)(2,1)}, bf16[128,1024]{0,1:T(8,128)(2,1)}, u32[]{:S(2)}, u32[]{:S(2)}) collective-permute-start(bf16[128,1024]{0,1:T(8,128)(2,1)} %bitcast.46), channel_id=1, source_target_pairs={{32,0},{36,4},{40,8},{44,12},{48,16},{52,20},{56,24},{60,28},{64,3... | collective-permute-start | bytes 786440 | tf_op jit(solution)/shard_map/ppermute | solution.py:36
  774.1 64.3 %collective-permute-start.16 = (bf16[128,1024]{0,1:T(8,128)(2,1)}, bf16[128,1024]{0,1:T(8,128)(2,1)}, u32[]{:S(2)}, u32[]{:S(2)}) collective-permute-start(bf16[128,1024]{0,1:T(8,128)(2,1)} %bitcast.39), channel_id=1, source_target_pairs={{4,0},{8,4},{12,8},{16,12},{20,16},{24,20},{28,24},{32,28},{36,32}... | collective-permute-start | bytes 786440 | tf_op jit(solution)/shard_map/ppermute | solution.py:36
  783.8 56.5 %collective-permute-start.22 = (bf16[128,1024]{0,1:T(8,128)(2,1)}, bf16[128,1024]{0,1:T(8,128)(2,1)}, u32[]{:S(2)}, u32[]{:S(2)}) collective-permute-start(bf16[128,1024]{0,1:T(8,128)(2,1)} %bitcast.45), channel_id=1, source_target_pairs={{28,0},{32,4},{36,8},{40,12},{44,16},{48,20},{52,24},{56,28},{60,3... | collective-permute-start | bytes 786440 | tf_op jit(solution)/shard_map/ppermute | solution.py:36
  789.6 74.3 %collective-permute-start.21 = (bf16[128,1024]{0,1:T(8,128)(2,1)}, bf16[128,1024]{0,1:T(8,128)(2,1)S(1)}, u32[]{:S(2)}, u32[]{:S(2)}) collective-permute-start(bf16[128,1024]{0,1:T(8,128)(2,1)} %bitcast.278), channel_id=1, source_target_pairs={{24,0},{28,4},{32,8},{36,12},{40,16},{44,20},{48,24},{52,28},{56,3... | collective-permute-start | bytes 786440 | tf_op jit(solution)/shard_map/ppermute | solution.py:36
  791.5 74.3 %collective-permute-start.20 = (bf16[128,1024]{0,1:T(8,128)(2,1)}, bf16[128,1024]{0,1:T(8,128)(2,1)S(1)}, u32[]{:S(2)}, u32[]{:S(2)}) collective-permute-start(bf16[128,1024]{0,1:T(8,128)(2,1)} %bitcast.277), channel_id=1, source_target_pairs={{20,0},{24,4},{28,8},{32,12},{36,16},{40,20},{44,24},{48,28},{52,3... | collective-permute-start | bytes 786440 | tf_op jit(solution)/shard_map/ppermute | solution.py:36
  793.4 74.3 %collective-permute-start.19 = (bf16[128,1024]{0,1:T(8,128)(2,1)}, bf16[128,1024]{0,1:T(8,128)(2,1)S(1)}, u32[]{:S(2)}, u32[]{:S(2)}) collective-permute-start(bf16[128,1024]{0,1:T(8,128)(2,1)} %bitcast.276), channel_id=1, source_target_pairs={{16,0},{20,4},{24,8},{28,12},{32,16},{36,20},{40,24},{44,28},{48,3... | collective-permute-start | bytes 786440 | tf_op jit(solution)/shard_map/ppermute | solution.py:36
  838.4 31.3 %collective-permute-start.18 = (bf16[128,1024]{0,1:T(8,128)(2,1)}, bf16[128,1024]{0,1:T(8,128)(2,1)}, u32[]{:S(2)}, u32[]{:S(2)}) collective-permute-start(bf16[128,1024]{0,1:T(8,128)(2,1)} %bitcast.275), channel_id=1, source_target_pairs={{12,0},{16,4},{20,8},{24,12},{28,16},{32,20},{36,24},{40,28},{44,3... | collective-permute-start | bytes 786440 | tf_op jit(solution)/shard_map/ppermute | solution.py:36
  840.3 51.0 %collective-permute-start.17 = (bf16[128,1024]{0,1:T(8,128)(2,1)}, bf16[128,1024]{0,1:T(8,128)(2,1)}, u32[]{:S(2)}, u32[]{:S(2)}) collective-permute-start(bf16[128,1024]{0,1:T(8,128)(2,1)} %bitcast.274), channel_id=1, source_target_pairs={{8,0},{12,4},{16,8},{20,12},{24,16},{28,20},{32,24},{36,28},{40,32... | collective-permute-start | bytes 786440 | tf_op jit(solution)/shard_map/ppermute | solution.py:36
  857.0 36.2 %copy-start.7 = (f32[128,4,2,128]{0,3,2,1:T(8,128)S(1)}, f32[128,4,2,128]{0,3,2,1:T(8,128)}, u32[]{:S(2)}) copy-start(f32[128,4,2,128]{0,3,2,1:T(8,128)} %slice.144) | copy-start | bytes 1572868
  863.9 50.8 %collective-permute-start.25 = (bf16[128,1024]{1,0:T(8,128)(2,1)}, bf16[128,1024]{1,0:T(8,128)(2,1)}, u32[]{:S(2)}, u32[]{:S(2)}) collective-permute-start(bf16[128,1024]{1,0:T(8,128)(2,1)} %copy.218), channel_id=1, source_target_pairs={{8,0},{12,4},{16,8},{20,12},{24,16},{28,20},{32,24},{36,28},{40,32... | collective-permute-start | bytes 786440 | tf_op jit(solution)/shard_map/ppermute | solution.py:36
  865.8 53.4 %collective-permute-start.26 = (bf16[128,1024]{1,0:T(8,128)(2,1)}, bf16[128,1024]{1,0:T(8,128)(2,1)}, u32[]{:S(2)}, u32[]{:S(2)}) collective-permute-start(bf16[128,1024]{1,0:T(8,128)(2,1)} %copy.219), channel_id=1, source_target_pairs={{12,0},{16,4},{20,8},{24,12},{28,16},{32,20},{36,24},{40,28},{44,3... | collective-permute-start | bytes 786440 | tf_op jit(solution)/shard_map/ppermute | solution.py:36
  867.7 55.9 %collective-permute-start.27 = (bf16[128,1024]{1,0:T(8,128)(2,1)}, bf16[128,1024]{1,0:T(8,128)(2,1)}, u32[]{:S(2)}, u32[]{:S(2)}) collective-permute-start(bf16[128,1024]{1,0:T(8,128)(2,1)} %copy.220), channel_id=1, source_target_pairs={{16,0},{20,4},{24,8},{28,12},{32,16},{36,20},{40,24},{44,28},{48,3... | collective-permute-start | bytes 786440 | tf_op jit(solution)/shard_map/ppermute | solution.py:36
  869.7 452.9 %collective-permute-start.28 = (bf16[128,1024]{1,0:T(8,128)(2,1)}, bf16[128,1024]{1,0:T(8,128)(2,1)}, u32[]{:S(2)}, u32[]{:S(2)}) collective-permute-start(bf16[128,1024]{1,0:T(8,128)(2,1)} %copy.221), channel_id=1, source_target_pairs={{20,0},{24,4},{28,8},{32,12},{36,16},{40,20},{44,24},{48,28},{52,3... | collective-permute-start | bytes 786440 | tf_op jit(solution)/shard_map/ppermute | solution.py:36
  891.3 431.3 %collective-permute-start.29 = (bf16[128,1024]{1,0:T(8,128)(2,1)}, bf16[128,1024]{1,0:T(8,128)(2,1)}, u32[]{:S(2)}, u32[]{:S(2)}) collective-permute-start(bf16[128,1024]{1,0:T(8,128)(2,1)} %copy.222), channel_id=1, source_target_pairs={{24,0},{28,4},{32,8},{36,12},{40,16},{44,20},{48,24},{52,28},{56,3... | collective-permute-start | bytes 786440 | tf_op jit(solution)/shard_map/ppermute | solution.py:36
  895.3 23.8 %copy-start.21 = (bf16[128,1024]{1,0:T(8,128)(2,1)S(1)}, bf16[128,1024]{1,0:T(8,128)(2,1)}, u32[]{:S(2)}) copy-start(bf16[128,1024]{1,0:T(8,128)(2,1)} %copy.224) | copy-start | bytes 786436
  895.3 28.3 %copy-start.20 = (bf16[128,1024]{1,0:T(8,128)(2,1)S(1)}, bf16[128,1024]{1,0:T(8,128)(2,1)}, u32[]{:S(2)}) copy-start(bf16[128,1024]{1,0:T(8,128)(2,1)} %copy.217) | copy-start | bytes 786436
  895.3 38.7 %copy-start.25 = (f32[128,8]{0,1:T(8,128)S(1)}, f32[128,8]{0,1:T(8,128)}, u32[]{:S(2)}) copy-start(f32[128,8]{0,1:T(8,128)} %copy-done.24) | copy-start | bytes 12292
  895.8 426.8 %copy-start.6 = (f32[128,1024]{1,0:T(8,128)S(1)}, f32[128,1024]{1,0:T(8,128)}, u32[]{:S(2)}) copy-start(f32[128,1024]{1,0:T(8,128)} %copy.216) | copy-start | bytes 1572868
  914.6 408.0 %collective-permute-start.30 = (bf16[128,1024]{1,0:T(8,128)(2,1)}, bf16[128,1024]{1,0:T(8,128)(2,1)S(1)}, u32[]{:S(2)}, u32[]{:S(2)}) collective-permute-start(bf16[128,1024]{1,0:T(8,128)(2,1)} %copy.223), channel_id=1, source_target_pairs={{28,0},{32,4},{36,8},{40,12},{44,16},{48,20},{52,24},{56,28},{60,3... | collective-permute-start | bytes 786440 | tf_op jit(solution)/shard_map/ppermute | solution.py:36
  919.2 403.4 %collective-permute-start.31 = (bf16[128,1024]{1,0:T(8,128)(2,1)S(1)}, bf16[128,1024]{1,0:T(8,128)(2,1)}, u32[]{:S(2)}, u32[]{:S(2)}) collective-permute-start(bf16[128,1024]{1,0:T(8,128)(2,1)S(1)} %copy-done.21), channel_id=1, source_target_pairs={{32,0},{36,4},{40,8},{44,12},{48,16},{52,20},{56,24},{60,28},{64,3... | collective-permute-start | bytes 786440 | tf_op jit(solution)/shard_map/ppermute | solution.py:36
  923.6 399.0 %collective-permute-start.24 = (bf16[128,1024]{1,0:T(8,128)(2,1)S(1)}, bf16[128,1024]{1,0:T(8,128)(2,1)}, u32[]{:S(2)}, u32[]{:S(2)}) collective-permute-start(bf16[128,1024]{1,0:T(8,128)(2,1)S(1)} %copy-done.20), channel_id=1, source_target_pairs={{4,0},{8,4},{12,8},{16,12},{20,16},{24,20},{28,24},{32,28},{36,32}... | collective-permute-start | bytes 786440 | tf_op jit(solution)/shard_map/ppermute | solution.py:36
  (21 other events, 28.8 us)
